TPU v7x, 512 devices: a whole 4x8x8 slice. The times are simulated.
512 devices in a mesh: grid: 64 (over x, z, core), orb: 8 (over y).
Axes of the slice: x: 4, y: 8, z: 8, core: 2. Of those that a mesh axis runs over, the one named last changes fastest.
Arguments:
- orbitals: float32 [256, 16, 16, 1024], P('grid', None, None, 'orb'), may hold values from -15 to 15
- potential: float32 [256, 16, 16], P('grid'), may hold values from -2 to 0
Outputs:
- filtered: float32 [256, 16, 16, 1024], P('grid', None, None, 'orb')
- hamiltonian_block: float32 [1024, 1024], P('orb', 'grid')
- margin_block: float32 [1024, 1024], P('orb', 'grid')
All inputs are finite; a program needn't handle non-finite values.
Results may differ from a plain program's by a relative error of at most 0.0039.
Values may be sent and summed in bfloat16 or wider, within the bound.
No kernel may reach another device: no remote copies, remote signals or barrier semaphores. Data moves between devices by JAX's collectives and lax.ppermute only.
A program may use at most 64 MiB of HBM per device.

v0:
```python
import jax
import jax.numpy as jnp
from jax import lax
from jax.sharding import PartitionSpec as P

DEGREE = 4
STENCIL = (-205.0 / 72.0, 8.0 / 5.0, -1.0 / 5.0, 8.0 / 315.0, -1.0 / 560.0)
LOWER_EDGE = -2.0
CUT_EDGE = 1.5
UPPER_EDGE = 10.0
EPSILON = 1e-06


def padded_2(shard, sides, width):
    for axis, dim in sides:
        size, length = (lax.axis_size(axis), shard.shape[dim])
        up = [(i, (i + 1) % size) for i in range(size - 1)]
        down = [(j, i) for i, j in up]
        last = lax.slice_in_dim(shard, length - width, length, axis=dim)
        initial = lax.slice_in_dim(shard, 0, width, axis=dim)
        before = lax.ppermute(last, axis, up)
        after = lax.ppermute(initial, axis, down)
        shard = jnp.concatenate([before, shard, after], axis=dim)
    return shard


def plane_matrix(rows_y, cols_x):
    flat_count = rows_y * cols_x
    index_all = jnp.arange(flat_count, dtype=jnp.int32)
    row_y = (index_all // cols_x)[:, None]
    row_x = (index_all % cols_x)[:, None]
    col_y = (index_all // cols_x)[None, :]
    col_x = (index_all % cols_x)[None, :]
    delta_y = jnp.mod(row_y - col_y, rows_y)
    delta_x = jnp.mod(row_x - col_x, cols_x)
    same_y = delta_y == 0
    same_x = delta_x == 0
    matrix = jnp.zeros((flat_count, flat_count), jnp.float32)
    for offset in range(1, 5):
        for signed in (offset, -offset):
            hit_y = jnp.logical_and(same_x, delta_y == signed % rows_y)
            hit_x = jnp.logical_and(same_y, delta_x == signed % cols_x)
            matrix = matrix + STENCIL[offset] * (
                hit_y.astype(jnp.float32) + hit_x.astype(jnp.float32)
            )
    return matrix


def apply_hamiltonian(current, potential, plane):
    layers, rows_y, cols_x, width = current.shape
    padded = padded_2(current.astype(jnp.bfloat16), (("grid", 0),), 4).astype(current.dtype)
    laplacian = 3.0 * STENCIL[0] * current
    for offset in range(1, 5):
        laplacian = laplacian + STENCIL[offset] * (
            padded[4 + offset : 4 + offset + layers] + padded[4 - offset : 4 - offset + layers]
        )
    flat = current.reshape(layers, rows_y * cols_x, width)
    in_plane = jnp.einsum(
        "pq,zqo->zpo",
        plane,
        flat,
        precision=lax.Precision.HIGHEST,
        preferred_element_type=jnp.float32,
    )
    laplacian = laplacian + in_plane.reshape(current.shape)
    return -0.5 * laplacian + potential[:, :, :, None] * current


def chebyshev(initial, potential, plane):
    half_width = (UPPER_EDGE - CUT_EDGE) / 2.0
    centre = (UPPER_EDGE + CUT_EDGE) / 2.0
    sigma_now = half_width / (LOWER_EDGE - centre)
    gamma_ratio = 2.0 / sigma_now
    previous = initial
    current = (
        sigma_now / half_width * (apply_hamiltonian(previous, potential, plane) - centre * previous)
    )
    for degree_step in range(DEGREE - 1):
        sigma_next = 1.0 / (gamma_ratio - sigma_now)
        following = (
            2.0
            * sigma_next
            / half_width
            * (apply_hamiltonian(current, potential, plane) - centre * current)
            - sigma_now * sigma_next * previous
        )
        previous, current, sigma_now = (current, following, sigma_next)
    return current


def contract_points(left_side, right_side):
    return lax.dot_general(
        left_side, right_side, (((0,), (0,)), ((), ())), preferred_element_type=jnp.float32
    )


def on_device(orbitals, potential):
    own_width = orbitals.shape[3]
    point_count = orbitals.shape[0] * orbitals.shape[1] * orbitals.shape[2]
    point_total = float(point_count * lax.axis_size("grid"))
    plane = plane_matrix(orbitals.shape[1], orbitals.shape[2])
    result_block = chebyshev(orbitals, potential, plane)
    own_squares = jnp.sum(result_block * result_block, axis=(0, 1, 2))
    rounded_orbitals = result_block.astype(jnp.bfloat16).reshape(point_count, own_width)
    rounded_image = (
        apply_hamiltonian(result_block, potential, plane)
        .astype(jnp.bfloat16)
        .reshape(point_count, own_width)
    )
    summed_own = lax.psum(own_squares, "grid")
    squares_all = lax.all_gather(summed_own, "orb", axis=0, tiled=True)
    scale_all = 1.0 / jnp.sqrt(squares_all / point_total + EPSILON)
    scale_own = lax.dynamic_slice_in_dim(scale_all, lax.axis_index("orb") * own_width, own_width)
    filtered = result_block * scale_own
    orbitals_all, images_all = (
        lax.all_gather(rounded_orbitals, "orb", axis=1, tiled=True),
        lax.all_gather(rounded_image, "orb", axis=1, tiled=True),
    )
    hamiltonian_part = contract_points(images_all, rounded_orbitals)
    margin_part = contract_points(orbitals_all, rounded_orbitals)
    combined = lax.psum_scatter(
        jnp.concatenate([hamiltonian_part, margin_part], axis=1),
        "grid",
        scatter_dimension=0,
        tiled=True,
    )
    column_count = combined.shape[0]
    column_scale = lax.dynamic_slice_in_dim(
        scale_all, lax.axis_index("grid") * column_count, column_count
    )
    pair_scale = scale_own[:, None] * column_scale[None, :] / point_total
    hamiltonian_block = combined[:, :own_width].T * pair_scale
    margin_block = combined[:, own_width:].T * pair_scale
    return (filtered, hamiltonian_block, margin_block)


def solution(mesh):
    placed = (P("grid", None, None, "orb"), P("grid", None, None))
    return jax.shard_map(
        on_device,
        mesh=mesh,
        in_specs=placed,
        out_specs=(P("grid", None, None, "orb"), P("orb", "grid"), P("orb", "grid")),
        check_vma=False,
    )
```

profile of v0, /device:TPU:8, one launch (start us, length us, event | category | flops | bytes accessed | tf_op | source)
XLA Modules:
  0.0 412.1 jit_solution(13175780743739567016)
XLA Ops:
  7.2 1.1 convert_element_type.210
  8.3 1.3 collective-permute-start.1
  9.6 3.0 collective-permute-start
  12.7 0.8 broadcast_multiply_fusion.2
  13.4 2.7 fusion.72
  16.3 0.9 copy-done.1
  17.5 1.3 collective-permute-start.3
  18.8 4.5 %collective-permute-start.2 = (bf16[4,16,16,128]{3,2,1,0:T(8,128)(2,1)S(1)}, bf16[4,16,16,128]{3,2,1,0:T(8,128)(2,1)S(1)}, u32[]{:S(2)}, u32[]{:S(2)}) collective-permute-start(bf16[4,16,16,128]{3,2,1,0:T(8,128)(2,1)S(1)} %get-tuple-element.18), channel_id=1, source_target_pairs={{0,8},{8,16},{16,24},{24,32},{32,40},{40,48},{48,56},{56,64},{64,7... | collective-permute-start | bytes 786440 | tf_op jit(solution)/shard_map/ppermute | solution.py:21
  23.4 1.9 convolution_bitcast_fusion.3
  25.7 0.4 fusion.160
  26.2 1.3 collective-permute-start.5
  27.5 5.3 %collective-permute-start.4 = (bf16[4,16,16,128]{3,2,1,0:T(8,128)(2,1)S(1)}, bf16[4,16,16,128]{3,2,1,0:T(8,128)(2,1)S(1)}, u32[]{:S(2)}, u32[]{:S(2)}) collective-permute-start(bf16[4,16,16,128]{3,2,1,0:T(8,128)(2,1)S(1)} %get-tuple-element.16), channel_id=1, source_target_pairs={{0,8},{8,16},{16,24},{24,32},{32,40},{40,48},{48,56},{56,64},{64,7... | collective-permute-start | bytes 786440 | tf_op jit(solution)/shard_map/ppermute | solution.py:21
  32.8 1.9 convolution_bitcast_fusion.2
  35.1 0.4 fusion.158
  35.5 1.3 collective-permute-start.7
  36.8 6.2 %collective-permute-start.6 = (bf16[4,16,16,128]{3,2,1,0:T(8,128)(2,1)S(1)}, bf16[4,16,16,128]{3,2,1,0:T(8,128)(2,1)S(1)}, u32[]{:S(2)}, u32[]{:S(2)}) collective-permute-start(bf16[4,16,16,128]{3,2,1,0:T(8,128)(2,1)S(1)} %get-tuple-element.14), channel_id=1, source_target_pairs={{0,8},{8,16},{16,24},{24,32},{32,40},{40,48},{48,56},{56,64},{64,7... | collective-permute-start | bytes 786440 | tf_op jit(solution)/shard_map/ppermute | solution.py:21
  43.0 1.9 convolution_bitcast_fusion.1
  45.3 1.2 fusion.156
  46.5 1.3 collective-permute-start.9
  47.8 6.3 %collective-permute-start.8 = (bf16[4,16,16,128]{3,2,1,0:T(8,128)(2,1)}, bf16[4,16,16,128]{3,2,1,0:T(8,128)(2,1)S(1)}, u32[]{:S(2)}, u32[]{:S(2)}) collective-permute-start(bf16[4,16,16,128]{3,2,1,0:T(8,128)(2,1)} %get-tuple-element.12), channel_id=1, source_target_pairs={{0,8},{8,16},{16,24},{24,32},{32,40},{40,48},{48,56},{56,64},{64,7... | collective-permute-start | bytes 786440 | tf_op jit(solution)/shard_map/ppermute | solution.py:21
  54.1 1.9 convolution_bitcast_fusion
  56.4 134.8 %psum.7 = f32[128]{0:T(128)S(1)} all-reduce(f32[128]{0:T(128)S(1)} %multiply_reduce_fusion), channel_id=1, replica_groups=mesh['grid'=64,'orb'=8] {'grid'}, use_global_device_ids=true, to_apply=%region_1.2 | all-reduce | flops 128 | bytes 1024 | tf_op jit(solution)/shard_map/psum | solution.py:110
  191.2 15.3 %all-gather = f32[8,1,128]{2,1,0:T(1,128)S(1)} all-gather(f32[1,1,128]{2,1,0:T(1,128)S(1)} %bitcast.65), channel_id=1, replica_groups=mesh['grid'=64,'orb'=8] {'orb'}, dimensions={0}, use_global_device_ids=true | all-gather | bytes 4608 | tf_op jit(solution)/shard_map/all_gather | solution.py:111
  206.7 1.3 fusion.5
  208.1 2.1 fusion.165
  210.2 39.9 %all-gather.4.cloned.1.call-done = bf16[1024,1024]{1,0:T(8,128)(2,1)} async-done(((bf16[1024,128]{1,0:T(8,128)(2,1)}), bf16[1024,1024]{1,0:T(8,128)(2,1)}) %all-gather.4.cloned.1.call-update) | async-done | bytes 2097168 | tf_op jit(solution)/shard_map/all_gather | solution.py:117
  250.1 2.1 fusion.164
  252.2 1.3 copy.39
  253.7 149.6 %reduce-scatter.4.cloned.1.call-done = f32[16,256]{1,0:T(8,128)} async-done(((f32[1024,256]{1,0:T(8,128)}), f32[16,256]{1,0:T(8,128)}) %reduce-scatter.4.cloned.1.call-update) | async-done | bytes 16400
  403.3 0.7 fusion.163
  404.3 0.7 copy.33
  404.9 0.7 copy.34
  (42 shorter events, 2.7 us)
Async XLA Ops:
  7.2 200.9 %all-gather.6.cloned.1.call-start = ((), (), s32[]{:S(2)}) async-start(), calls=%async_computation.2 | async-start | bytes 2359296 | tf_op jit(solution)/shard_map/all_gather | solution.py:116
  8.3 7.8 %collective-permute-start.1 = (bf16[4,16,16,128]{3,2,1,0:T(8,128)(2,1)S(1)}, bf16[4,16,16,128]{3,2,1,0:T(8,128)(2,1)S(1)}, u32[]{:S(2)}, u32[]{:S(2)}) collective-permute-start(bf16[4,16,16,128]{3,2,1,0:T(8,128)(2,1)S(1)} %convert_element_type.210), channel_id=1, source_target_pairs={{8,0},{16,8},{24,16},{32,24},{40,32},{48,40},{56,48},{64,56},{72,6... | collective-permute-start | bytes 786440 | tf_op jit(solution)/shard_map/ppermute | solution.py:22
  9.6 6.5 %collective-permute-start = (bf16[4,16,16,128]{3,2,1,0:T(8,128)(2,1)S(1)}, bf16[4,16,16,128]{3,2,1,0:T(8,128)(2,1)S(1)}, u32[]{:S(2)}, u32[]{:S(2)}) collective-permute-start(bf16[4,16,16,128]{3,2,1,0:T(8,128)(2,1)S(1)} %convert_element_type.210), channel_id=1, source_target_pairs={{0,8},{8,16},{16,24},{24,32},{32,40},{40,48},{48,56},{56,64},{64,7... | collective-permute-start | bytes 786440 | tf_op jit(solution)/shard_map/ppermute | solution.py:21
  16.1 1.0 copy-start.1
  16.1 1.0 copy-start.2
  17.5 8.0 %collective-permute-start.3 = (bf16[4,16,16,128]{3,2,1,0:T(8,128)(2,1)S(1)}, bf16[4,16,16,128]{3,2,1,0:T(8,128)(2,1)S(1)}, u32[]{:S(2)}, u32[]{:S(2)}) collective-permute-start(bf16[4,16,16,128]{3,2,1,0:T(8,128)(2,1)S(1)} %get-tuple-element.18), channel_id=1, source_target_pairs={{8,0},{16,8},{24,16},{32,24},{40,32},{48,40},{56,48},{64,56},{72,6... | collective-permute-start | bytes 786440 | tf_op jit(solution)/shard_map/ppermute | solution.py:22
  18.8 6.7 %collective-permute-start.2 = (bf16[4,16,16,128]{3,2,1,0:T(8,128)(2,1)S(1)}, bf16[4,16,16,128]{3,2,1,0:T(8,128)(2,1)S(1)}, u32[]{:S(2)}, u32[]{:S(2)}) collective-permute-start(bf16[4,16,16,128]{3,2,1,0:T(8,128)(2,1)S(1)} %get-tuple-element.18), channel_id=1, source_target_pairs={{0,8},{8,16},{16,24},{24,32},{32,40},{40,48},{48,56},{56,64},{64,7... | collective-permute-start | bytes 786440 | tf_op jit(solution)/shard_map/ppermute | solution.py:21
  26.2 8.8 %collective-permute-start.5 = (bf16[4,16,16,128]{3,2,1,0:T(8,128)(2,1)S(1)}, bf16[4,16,16,128]{3,2,1,0:T(8,128)(2,1)S(1)}, u32[]{:S(2)}, u32[]{:S(2)}) collective-permute-start(bf16[4,16,16,128]{3,2,1,0:T(8,128)(2,1)S(1)} %get-tuple-element.16), channel_id=1, source_target_pairs={{8,0},{16,8},{24,16},{32,24},{40,32},{48,40},{56,48},{64,56},{72,6... | collective-permute-start | bytes 786440 | tf_op jit(solution)/shard_map/ppermute | solution.py:22
  27.5 7.5 %collective-permute-start.4 = (bf16[4,16,16,128]{3,2,1,0:T(8,128)(2,1)S(1)}, bf16[4,16,16,128]{3,2,1,0:T(8,128)(2,1)S(1)}, u32[]{:S(2)}, u32[]{:S(2)}) collective-permute-start(bf16[4,16,16,128]{3,2,1,0:T(8,128)(2,1)S(1)} %get-tuple-element.16), channel_id=1, source_target_pairs={{0,8},{8,16},{16,24},{24,32},{32,40},{40,48},{48,56},{56,64},{64,7... | collective-permute-start | bytes 786440 | tf_op jit(solution)/shard_map/ppermute | solution.py:21
  35.5 9.6 %collective-permute-start.7 = (bf16[4,16,16,128]{3,2,1,0:T(8,128)(2,1)S(1)}, bf16[4,16,16,128]{3,2,1,0:T(8,128)(2,1)S(1)}, u32[]{:S(2)}, u32[]{:S(2)}) collective-permute-start(bf16[4,16,16,128]{3,2,1,0:T(8,128)(2,1)S(1)} %get-tuple-element.14), channel_id=1, source_target_pairs={{8,0},{16,8},{24,16},{32,24},{40,32},{48,40},{56,48},{64,56},{72,6... | collective-permute-start | bytes 786440 | tf_op jit(solution)/shard_map/ppermute | solution.py:22
  36.8 8.3 %collective-permute-start.6 = (bf16[4,16,16,128]{3,2,1,0:T(8,128)(2,1)S(1)}, bf16[4,16,16,128]{3,2,1,0:T(8,128)(2,1)S(1)}, u32[]{:S(2)}, u32[]{:S(2)}) collective-permute-start(bf16[4,16,16,128]{3,2,1,0:T(8,128)(2,1)S(1)} %get-tuple-element.14), channel_id=1, source_target_pairs={{0,8},{8,16},{16,24},{24,32},{32,40},{40,48},{48,56},{56,64},{64,7... | collective-permute-start | bytes 786440 | tf_op jit(solution)/shard_map/ppermute | solution.py:21
  46.4 203.6 %all-gather.4.cloned.1.call-start = ((), (), s32[]{:S(2)}) async-start(), calls=%async_computation.1 | async-start | bytes 2359296 | tf_op jit(solution)/shard_map/all_gather | solution.py:117
  46.5 160.1 %collective-permute-start.9 = (bf16[4,16,16,128]{3,2,1,0:T(8,128)(2,1)}, bf16[4,16,16,128]{3,2,1,0:T(8,128)(2,1)S(1)}, u32[]{:S(2)}, u32[]{:S(2)}) collective-permute-start(bf16[4,16,16,128]{3,2,1,0:T(8,128)(2,1)} %get-tuple-element.12), channel_id=1, source_target_pairs={{8,0},{16,8},{24,16},{32,24},{40,32},{48,40},{56,48},{64,56},{72,6... | collective-permute-start | bytes 786440 | tf_op jit(solution)/shard_map/ppermute | solution.py:22
  47.8 158.8 %collective-permute-start.8 = (bf16[4,16,16,128]{3,2,1,0:T(8,128)(2,1)}, bf16[4,16,16,128]{3,2,1,0:T(8,128)(2,1)S(1)}, u32[]{:S(2)}, u32[]{:S(2)}) collective-permute-start(bf16[4,16,16,128]{3,2,1,0:T(8,128)(2,1)} %get-tuple-element.12), channel_id=1, source_target_pairs={{0,8},{8,16},{16,24},{24,32},{32,40},{40,48},{48,56},{56,64},{64,7... | collective-permute-start | bytes 786440 | tf_op jit(solution)/shard_map/ppermute | solution.py:21
  56.1 150.5 %copy-start = (bf16[4,16,16,128]{3,2,1,0:T(8,128)(2,1)S(1)}, bf16[4,16,16,128]{3,2,1,0:T(8,128)(2,1)}, u32[]{:S(2)}) copy-start(bf16[4,16,16,128]{3,2,1,0:T(8,128)(2,1)} %get-tuple-element.12) | copy-start | bytes 786436
  208.0 195.2 %reduce-scatter.4.cloned.1.call-start = ((), (), s32[]{:S(2)}) async-start(), calls=%async_computation.3 | async-start | bytes 1064960
Sparse Core Ops, SparseCore 0:
  46.6 66.5 all-gather.5
  208.2 41.8 all-gather.3
  254.6 148.5 reduce-scatter.3
where the time goes:
time: 413 us; the launch traced here: 412 us
  waiting for transfers between devices  190 us (46%)
  blocking collectives  150 us (36%)
  starting transfers between devices  32 us (8%)
  matrix products  14.5 us (4%)
  between operations  14.1 us (3%)
  other arithmetic  6.55 us (2%)
  local copies, waits for them, and re-layouts  5.38 us (1%)
    unnamed x4, waiting for transfers between devices  150 us
    psum x1, blocking collectives, on_device(): summed_own = lax.psum(own_squares, 'grid')  135 us
    all_gather x1, waiting for transfers between devices, on_device(): lax.all_gather(rounded_image, 'orb', axis=1, tiled=True)  39.9 us
    ppermute x5, starting transfers between devices, padded_2(): before = lax.ppermute(last, axis, up)  25.4 us
    all_gather x1, blocking collectives, on_device(): squares_all = lax.all_gather(summed_own, 'orb', axis=0, tiled=True)  15.3 us
    dot_general x5, matrix products, apply_hamiltonian(): jnp.einsum('pq,zqo->zpo', plane, flat, precision=lax.Precision.HIGHEST, p...  10.4 us
  transfers between devices with their start and end apart: 13, of which 2 were waited for; matrix products, arithmetic and copies ran while one was open for 4% of the time, Pallas kernels for 0%

commit v1 on v0

--- a/solution.py
+++ b/solution.py
@@ -107,7 +107,7 @@
         .astype(jnp.bfloat16)
         .reshape(point_count, own_width)
     )
-    summed_own = lax.psum(own_squares, "grid")
+    summed_own = jnp.sum(lax.all_gather(own_squares, "grid"), axis=0)
     squares_all = lax.all_gather(summed_own, "orb", axis=0, tiled=True)
     scale_all = 1.0 / jnp.sqrt(squares_all / point_total + EPSILON)
     scale_own = lax.dynamic_slice_in_dim(scale_all, lax.axis_index("orb") * own_width, own_width)

time: 413 us -> 338 us (0.82)
  blocking collectives: 150 us -> 71.1 us
    psum x1 -> x0, blocking collectives: 135 us -> none  [on_device(): summed_own = lax.psum(own_squares, 'grid')]
    all_gather x0 -> x1, blocking collectives: none -> 55.8 us  [on_device(): summed_own = jnp.sum(lax.all_gather(own_squares, 'grid'), axis=0)]
    all_gather x1, waiting for transfers between devices: 39.9 us -> 44.3 us  [on_device(): lax.all_gather(rounded_image, 'orb', axis=1, tiled=True)]
  transfers between devices with their start and end apart: 13 -> 13, of which waited for: 2 -> 2; matrix products, arithmetic and copies ran while one was open for 4% -> 5% of each run, Pallas kernels for 0% -> 0%
where the time goes in v1:
time: 338 us
  waiting for transfers between devices  194 us (57%)
  blocking collectives  71.1 us (21%)
  starting transfers between devices  32 us (9%)
  matrix products  14.5 us (4%)
  between operations  14.1 us (4%)
  other arithmetic  6.63 us (2%)
  local copies, waits for them, and re-layouts  5.38 us (2%)
    unnamed x4, waiting for transfers between devices  150 us
    all_gather x1, blocking collectives, on_device(): summed_own = jnp.sum(lax.all_gather(own_squares, 'grid'), axis=0)  55.8 us
    all_gather x1, waiting for transfers between devices, on_device(): lax.all_gather(rounded_image, 'orb', axis=1, tiled=True)  44.3 us
    ppermute x5, starting transfers between devices, padded_2(): before = lax.ppermute(last, axis, up)  25.4 us
    all_gather x1, blocking collectives, on_device(): squares_all = lax.all_gather(summed_own, 'orb', axis=0, tiled=True)  15.3 us
    dot_general x5, matrix products, apply_hamiltonian(): jnp.einsum('pq,zqo->zpo', plane, flat, precision=lax.Precision.HIGHEST, p...  10.4 us
  transfers between devices with their start and end apart: 13, of which 2 were waited for; matrix products, arithmetic and copies ran while one was open for 5% of the time, Pallas kernels for 0%

profile of v1, /device:TPU:8, one launch (start us, length us, event | category | flops | bytes accessed | tf_op | source)
XLA Modules:
  0.0 337.8 jit_solution(11831510645152667847)
XLA Ops:
  7.2 1.1 convert_element_type.210
  8.3 1.3 collective-permute-start.1
  9.6 3.0 collective-permute-start
  12.7 0.8 broadcast_multiply_fusion.2
  13.4 2.7 fusion.72
  16.3 0.9 copy-done.1
  17.5 1.3 collective-permute-start.3
  18.8 4.5 %collective-permute-start.2 = (bf16[4,16,16,128]{3,2,1,0:T(8,128)(2,1)S(1)}, bf16[4,16,16,128]{3,2,1,0:T(8,128)(2,1)S(1)}, u32[]{:S(2)}, u32[]{:S(2)}) collective-permute-start(bf16[4,16,16,128]{3,2,1,0:T(8,128)(2,1)S(1)} %get-tuple-element.18), channel_id=1, source_target_pairs={{0,8},{8,16},{16,24},{24,32},{32,40},{40,48},{48,56},{56,64},{64,7... | collective-permute-start | bytes 786440 | tf_op jit(solution)/shard_map/ppermute | solution.py:21
  23.4 1.9 convolution_bitcast_fusion.3
  25.7 0.4 fusion.160
  26.2 1.3 collective-permute-start.5
  27.5 5.3 %collective-permute-start.4 = (bf16[4,16,16,128]{3,2,1,0:T(8,128)(2,1)S(1)}, bf16[4,16,16,128]{3,2,1,0:T(8,128)(2,1)S(1)}, u32[]{:S(2)}, u32[]{:S(2)}) collective-permute-start(bf16[4,16,16,128]{3,2,1,0:T(8,128)(2,1)S(1)} %get-tuple-element.16), channel_id=1, source_target_pairs={{0,8},{8,16},{16,24},{24,32},{32,40},{40,48},{48,56},{56,64},{64,7... | collective-permute-start | bytes 786440 | tf_op jit(solution)/shard_map/ppermute | solution.py:21
  32.8 1.9 convolution_bitcast_fusion.2
  35.1 0.4 fusion.158
  35.5 1.3 collective-permute-start.7
  36.8 6.2 %collective-permute-start.6 = (bf16[4,16,16,128]{3,2,1,0:T(8,128)(2,1)S(1)}, bf16[4,16,16,128]{3,2,1,0:T(8,128)(2,1)S(1)}, u32[]{:S(2)}, u32[]{:S(2)}) collective-permute-start(bf16[4,16,16,128]{3,2,1,0:T(8,128)(2,1)S(1)} %get-tuple-element.14), channel_id=1, source_target_pairs={{0,8},{8,16},{16,24},{24,32},{32,40},{40,48},{48,56},{56,64},{64,7... | collective-permute-start | bytes 786440 | tf_op jit(solution)/shard_map/ppermute | solution.py:21
  43.0 1.9 convolution_bitcast_fusion.1
  45.3 1.2 fusion.156
  46.5 1.3 collective-permute-start.9
  47.8 6.3 %collective-permute-start.8 = (bf16[4,16,16,128]{3,2,1,0:T(8,128)(2,1)}, bf16[4,16,16,128]{3,2,1,0:T(8,128)(2,1)S(1)}, u32[]{:S(2)}, u32[]{:S(2)}) collective-permute-start(bf16[4,16,16,128]{3,2,1,0:T(8,128)(2,1)} %get-tuple-element.12), channel_id=1, source_target_pairs={{0,8},{8,16},{16,24},{24,32},{32,40},{40,48},{48,56},{56,64},{64,7... | collective-permute-start | bytes 786440 | tf_op jit(solution)/shard_map/ppermute | solution.py:21
  54.1 1.9 convolution_bitcast_fusion
  56.4 55.8 %all-gather.1 = f32[64,1,128]{2,1,0:T(1,128)S(1)} all-gather(f32[1,1,128]{2,1,0:T(1,128)S(1)} %bitcast.66), channel_id=2, replica_groups=mesh['grid'=64,'orb'=8] {'grid'}, dimensions={0}, use_global_device_ids=true | all-gather | bytes 33280 | tf_op jit(solution)/shard_map/all_gather | solution.py:110
  112.4 15.3 %all-gather.2 = f32[8,1,128]{2,1,0:T(1,128)S(1)} all-gather(f32[1,1,128]{2,1,0:T(1,128)S(1)} %bitcast.67), channel_id=1, replica_groups=mesh['grid'=64,'orb'=8] {'orb'}, dimensions={0}, use_global_device_ids=true | all-gather | bytes 4608 | tf_op jit(solution)/shard_map/all_gather | solution.py:111
  127.9 1.3 fusion.5
  129.3 2.1 fusion.165
  131.4 44.3 %all-gather.6.cloned.1.call-done = bf16[1024,1024]{1,0:T(8,128)(2,1)} async-done(((bf16[1024,128]{1,0:T(8,128)(2,1)}), bf16[1024,1024]{1,0:T(8,128)(2,1)}) %all-gather.6.cloned.1.call-update) | async-done | bytes 2097168 | tf_op jit(solution)/shard_map/all_gather | solution.py:117
  175.7 2.1 fusion.164
  177.9 1.3 copy.39
  179.3 149.6 %reduce-scatter.4.cloned.1.call-done = f32[16,256]{1,0:T(8,128)} async-done(((f32[1024,256]{1,0:T(8,128)}), f32[16,256]{1,0:T(8,128)}) %reduce-scatter.4.cloned.1.call-update) | async-done | bytes 16400
  328.9 0.7 fusion.163
  329.9 0.7 copy.33
  330.6 0.7 copy.34
  (43 shorter events, 2.8 us)
Async XLA Ops:
  7.2 122.1 %all-gather.8.cloned.1.call-start = ((), (), s32[]{:S(2)}) async-start(), calls=%async_computation.2 | async-start | bytes 2359296 | tf_op jit(solution)/shard_map/all_gather | solution.py:116
  8.3 7.8 %collective-permute-start.1 = (bf16[4,16,16,128]{3,2,1,0:T(8,128)(2,1)S(1)}, bf16[4,16,16,128]{3,2,1,0:T(8,128)(2,1)S(1)}, u32[]{:S(2)}, u32[]{:S(2)}) collective-permute-start(bf16[4,16,16,128]{3,2,1,0:T(8,128)(2,1)S(1)} %convert_element_type.210), channel_id=1, source_target_pairs={{8,0},{16,8},{24,16},{32,24},{40,32},{48,40},{56,48},{64,56},{72,6... | collective-permute-start | bytes 786440 | tf_op jit(solution)/shard_map/ppermute | solution.py:22
  9.6 6.5 %collective-permute-start = (bf16[4,16,16,128]{3,2,1,0:T(8,128)(2,1)S(1)}, bf16[4,16,16,128]{3,2,1,0:T(8,128)(2,1)S(1)}, u32[]{:S(2)}, u32[]{:S(2)}) collective-permute-start(bf16[4,16,16,128]{3,2,1,0:T(8,128)(2,1)S(1)} %convert_element_type.210), channel_id=1, source_target_pairs={{0,8},{8,16},{16,24},{24,32},{32,40},{40,48},{48,56},{56,64},{64,7... | collective-permute-start | bytes 786440 | tf_op jit(solution)/shard_map/ppermute | solution.py:21
  16.1 1.0 copy-start.1
  16.1 1.0 copy-start.2
  17.5 8.0 %collective-permute-start.3 = (bf16[4,16,16,128]{3,2,1,0:T(8,128)(2,1)S(1)}, bf16[4,16,16,128]{3,2,1,0:T(8,128)(2,1)S(1)}, u32[]{:S(2)}, u32[]{:S(2)}) collective-permute-start(bf16[4,16,16,128]{3,2,1,0:T(8,128)(2,1)S(1)} %get-tuple-element.18), channel_id=1, source_target_pairs={{8,0},{16,8},{24,16},{32,24},{40,32},{48,40},{56,48},{64,56},{72,6... | collective-permute-start | bytes 786440 | tf_op jit(solution)/shard_map/ppermute | solution.py:22
  18.8 6.7 %collective-permute-start.2 = (bf16[4,16,16,128]{3,2,1,0:T(8,128)(2,1)S(1)}, bf16[4,16,16,128]{3,2,1,0:T(8,128)(2,1)S(1)}, u32[]{:S(2)}, u32[]{:S(2)}) collective-permute-start(bf16[4,16,16,128]{3,2,1,0:T(8,128)(2,1)S(1)} %get-tuple-element.18), channel_id=1, source_target_pairs={{0,8},{8,16},{16,24},{24,32},{32,40},{40,48},{48,56},{56,64},{64,7... | collective-permute-start | bytes 786440 | tf_op jit(solution)/shard_map/ppermute | solution.py:21
  26.2 8.8 %collective-permute-start.5 = (bf16[4,16,16,128]{3,2,1,0:T(8,128)(2,1)S(1)}, bf16[4,16,16,128]{3,2,1,0:T(8,128)(2,1)S(1)}, u32[]{:S(2)}, u32[]{:S(2)}) collective-permute-start(bf16[4,16,16,128]{3,2,1,0:T(8,128)(2,1)S(1)} %get-tuple-element.16), channel_id=1, source_target_pairs={{8,0},{16,8},{24,16},{32,24},{40,32},{48,40},{56,48},{64,56},{72,6... | collective-permute-start | bytes 786440 | tf_op jit(solution)/shard_map/ppermute | solution.py:22
  27.5 7.5 %collective-permute-start.4 = (bf16[4,16,16,128]{3,2,1,0:T(8,128)(2,1)S(1)}, bf16[4,16,16,128]{3,2,1,0:T(8,128)(2,1)S(1)}, u32[]{:S(2)}, u32[]{:S(2)}) collective-permute-start(bf16[4,16,16,128]{3,2,1,0:T(8,128)(2,1)S(1)} %get-tuple-element.16), channel_id=1, source_target_pairs={{0,8},{8,16},{16,24},{24,32},{32,40},{40,48},{48,56},{56,64},{64,7... | collective-permute-start | bytes 786440 | tf_op jit(solution)/shard_map/ppermute | solution.py:21
  35.5 9.6 %collective-permute-start.7 = (bf16[4,16,16,128]{3,2,1,0:T(8,128)(2,1)S(1)}, bf16[4,16,16,128]{3,2,1,0:T(8,128)(2,1)S(1)}, u32[]{:S(2)}, u32[]{:S(2)}) collective-permute-start(bf16[4,16,16,128]{3,2,1,0:T(8,128)(2,1)S(1)} %get-tuple-element.14), channel_id=1, source_target_pairs={{8,0},{16,8},{24,16},{32,24},{40,32},{48,40},{56,48},{64,56},{72,6... | collective-permute-start | bytes 786440 | tf_op jit(solution)/shard_map/ppermute | solution.py:22
  36.8 8.3 %collective-permute-start.6 = (bf16[4,16,16,128]{3,2,1,0:T(8,128)(2,1)S(1)}, bf16[4,16,16,128]{3,2,1,0:T(8,128)(2,1)S(1)}, u32[]{:S(2)}, u32[]{:S(2)}) collective-permute-start(bf16[4,16,16,128]{3,2,1,0:T(8,128)(2,1)S(1)} %get-tuple-element.14), channel_id=1, source_target_pairs={{0,8},{8,16},{16,24},{24,32},{32,40},{40,48},{48,56},{56,64},{64,7... | collective-permute-start | bytes 786440 | tf_op jit(solution)/shard_map/ppermute | solution.py:21
  46.4 129.3 %all-gather.6.cloned.1.call-start = ((), (), s32[]{:S(2)}) async-start(), calls=%async_computation.1 | async-start | bytes 2359296 | tf_op jit(solution)/shard_map/all_gather | solution.py:117
  46.5 81.3 %collective-permute-start.9 = (bf16[4,16,16,128]{3,2,1,0:T(8,128)(2,1)}, bf16[4,16,16,128]{3,2,1,0:T(8,128)(2,1)S(1)}, u32[]{:S(2)}, u32[]{:S(2)}) collective-permute-start(bf16[4,16,16,128]{3,2,1,0:T(8,128)(2,1)} %get-tuple-element.12), channel_id=1, source_target_pairs={{8,0},{16,8},{24,16},{32,24},{40,32},{48,40},{56,48},{64,56},{72,6... | collective-permute-start | bytes 786440 | tf_op jit(solution)/shard_map/ppermute | solution.py:22
  47.8 80.0 %collective-permute-start.8 = (bf16[4,16,16,128]{3,2,1,0:T(8,128)(2,1)}, bf16[4,16,16,128]{3,2,1,0:T(8,128)(2,1)S(1)}, u32[]{:S(2)}, u32[]{:S(2)}) collective-permute-start(bf16[4,16,16,128]{3,2,1,0:T(8,128)(2,1)} %get-tuple-element.12), channel_id=1, source_target_pairs={{0,8},{8,16},{16,24},{24,32},{32,40},{40,48},{48,56},{56,64},{64,7... | collective-permute-start | bytes 786440 | tf_op jit(solution)/shard_map/ppermute | solution.py:21
  56.1 71.7 %copy-start = (bf16[4,16,16,128]{3,2,1,0:T(8,128)(2,1)S(1)}, bf16[4,16,16,128]{3,2,1,0:T(8,128)(2,1)}, u32[]{:S(2)}) copy-start(bf16[4,16,16,128]{3,2,1,0:T(8,128)(2,1)} %get-tuple-element.12) | copy-start | bytes 786436
  129.2 199.7 %reduce-scatter.4.cloned.1.call-start = ((), (), s32[]{:S(2)}) async-start(), calls=%async_computation.3 | async-start | bytes 1064960
Sparse Core Ops, SparseCore 0:
  46.6 66.1 all-gather.7
  129.3 46.3 all-gather.5
  180.3 148.5 reduce-scatter.3
